TPU v7x, 32 devices: a whole 2x2x4 slice. The times are simulated.
32 devices in a mesh: group: 2 (over y), sub: 4 (over z), tile: 2 (over x), rep: 2 (over core).
Axes of the slice: x: 2, y: 2, z: 4, core: 2. Of those that a mesh axis runs over, the one named last changes fastest.
Arguments:
- right_side: bfloat16 [16, 1024, 512], P(('group', 'sub', 'tile'), None, 'rep'), parts along dimension 0, may hold values from -6 to 6
- interface_inverse: bfloat16 [16, 1024, 1024], P(('group', 'sub', 'tile')), parts along dimension 0, may hold values from -0.1875 to 0.1875
- coupling: float32 [16, 2, 128], P(('group', 'sub', 'tile')), parts along dimension 0, may hold values from 0.5 to 2
- trace_rows: int32 [16, 2, 128], P(('group', 'sub', 'tile')), parts along dimension 0, may hold values from 0 to 1023
- deflation_basis: bfloat16 [16, 1024, 128], P(('group', 'sub', 'tile')), parts along dimension 0, may hold values from -0.375 to 0.375
- deflation_counts: int32 [16], P(('group', 'sub', 'tile')), parts along dimension 0, may hold values from 32 to 128, as said below
- coarse_inverse: bfloat16 [8, 2, 128, 4, 256], P('group', 'tile', 'rep', 'sub'), parts along dimension 0, may hold values from -0.25 to 0.25
Outputs:
- corrected_field: bfloat16 [16, 1024, 512], P(('group', 'sub', 'tile'), None, 'rep'), parts along dimension 0
There are 2 independent parts, one for each index of `group`. A program takes and returns all parts, laid end to end along the dimension named above; each array names one. Nothing has to cross between parts.
Inputs may be any that keep to these rules, and one draw needn't show every extreme that they name: `deflation_counts`: some subdomain has exactly 128 live deflation vectors.
All inputs are finite; a program needn't handle non-finite values.
Results may differ from a plain program's by a relative error of at most 0.035.
Values may be sent and summed in bfloat16 or wider, within the bound.
No kernel may reach another device: no remote copies, remote signals or barrier semaphores. Data moves between devices by JAX's collectives and lax.ppermute only.
A program may use at most 64 MiB of HBM per device.

v0:
```python
import jax
import jax.numpy as jnp
from jax import lax
from jax.sharding import PartitionSpec as P

ROUNDS = 2


def passed_along(shard, axis, by):
    peers = lax.axis_size(axis)
    pairs = [(i, i + by) for i in range(peers) if 0 <= i + by < peers]
    return lax.ppermute(shard, axis, pairs)


def add_columns(matrix, piece):
    return jnp.dot(matrix, piece, preferred_element_type=jnp.float32)


def local(
    right_side,
    interface_inverse,
    coupling,
    trace_rows,
    deflation_basis,
    deflation_counts,
    coarse_inverse,
):
    source = right_side[0].astype(jnp.float32)
    inverse = interface_inverse[0]
    iface_rows = inverse.shape[0]
    face_rows = coupling.shape[2]
    mode_cols = source.shape[1]
    slot_count = deflation_basis.shape[2]
    half_slots = coarse_inverse.shape[2]
    sub_count = lax.axis_size("sub")
    slot_ids = jnp.arange(slot_count, dtype=jnp.int32)
    masked_basis = jnp.where(
        slot_ids[None, :] < deflation_counts[0],
        deflation_basis[0],
        jnp.zeros((), deflation_basis.dtype),
    )
    coarse_block = coarse_inverse.reshape(sub_count * half_slots, coarse_inverse.shape[4])
    lower_gain = coupling[0, 0][:, None]
    upper_gain = coupling[0, 1][:, None]
    iterate = jnp.zeros((iface_rows, mode_cols), jnp.float32)
    for cycle_index in range(ROUNDS):
        lower_trace = iterate[trace_rows[0, 0]]
        upper_trace = iterate[trace_rows[0, 1]]
        from_lower = passed_along(upper_trace.astype(jnp.bfloat16), ("sub", "tile"), 1).astype(
            upper_trace.dtype
        )
        from_upper = passed_along(lower_trace.astype(jnp.bfloat16), ("sub", "tile"), -1).astype(
            lower_trace.dtype
        )
        lower_rows = source[:face_rows] + lower_gain * from_lower
        upper_rows = source[iface_rows - face_rows :] + upper_gain * from_upper
        boundary = jnp.concatenate(
            [lower_rows, source[face_rows : iface_rows - face_rows], upper_rows], axis=0
        ).astype(jnp.bfloat16)
        local_solve = jnp.dot(inverse, boundary, preferred_element_type=jnp.float32)
        defect = (local_solve - iterate).astype(jnp.bfloat16)
        projected = lax.dot_general(
            masked_basis, defect, (((0,), (0,)), ((), ())), preferred_element_type=jnp.float32
        ).astype(jnp.bfloat16)
        all_modes = lax.all_gather(projected, "rep", axis=1, tiled=True)
        partial_value = add_columns(
            coarse_block, lax.all_gather(all_modes, "tile", axis=0, tiled=True)
        )
        own_coarse = lax.psum_scatter(
            partial_value.astype(jnp.bfloat16), "sub", scatter_dimension=0, tiled=True
        )
        coarse_rows = lax.all_to_all(own_coarse, "rep", split_axis=1, concat_axis=0, tiled=True)
        iterate = local_solve + jnp.dot(
            masked_basis, coarse_rows, preferred_element_type=jnp.float32
        )
    return iterate.astype(jnp.bfloat16)[None]


def solution(mesh):
    placed = (
        P(("group", "sub", "tile"), None, "rep"),
        P(("group", "sub", "tile"), None, None),
        P(("group", "sub", "tile"), None, None),
        P(("group", "sub", "tile"), None, None),
        P(("group", "sub", "tile"), None, None),
        P(("group", "sub", "tile")),
        P("group", "tile", "rep", "sub", None),
    )
    return jax.shard_map(
        local,
        mesh=mesh,
        in_specs=placed,
        out_specs=P(("group", "sub", "tile"), None, "rep"),
        check_vma=False,
    )
```

profile of v0, /device:TPU:0, one launch (start us, length us, event | category | flops | bytes accessed | tf_op | source)
XLA Modules:
  0.0 124.2 jit_solution(14332137796741248323)
XLA Ops:
  8.3 4.8 %collective-permute-start = (bf16[128,256]{1,0:T(8,128)(2,1)S(1)}, bf16[128,256]{1,0:T(8,128)(2,1)S(1)}, u32[]{:S(2)}, u32[]{:S(2)}) collective-permute-start(bf16[128,256]{1,0:T(8,128)(2,1)S(1)} %gather_fusion), channel_id=1, source_target_pairs={{0,2},{2,4},{4,6},{6,8},{8,10},{10,12},{12,14},{1,3},{3,5},{5,7},{... | collective-permute-start | bytes 196616 | tf_op jit(solution)/shard_map/ppermute | solution.py:12
  14.0 1.3 %collective-permute-start.1 = (bf16[128,256]{1,0:T(8,128)(2,1)S(1)}, bf16[128,256]{1,0:T(8,128)(2,1)S(1)}, u32[]{:S(2)}, u32[]{:S(2)}) collective-permute-start(bf16[128,256]{1,0:T(8,128)(2,1)S(1)} %gather_fusion.1), channel_id=1, source_target_pairs={{2,0},{4,2},{6,4},{8,6},{10,8},{12,10},{14,12},{3,1},{5,3},{7,5},{... | collective-permute-start | bytes 196616 | tf_op jit(solution)/shard_map/ppermute | solution.py:12
  16.7 1.1 convert_element_type.57
  17.9 2.2 %collective-permute-done.1 = bf16[128,256]{1,0:T(8,128)(2,1)S(1)} collective-permute-done((bf16[128,256]{1,0:T(8,128)(2,1)S(1)}, bf16[128,256]{1,0:T(8,128)(2,1)S(1)}, u32[]{:S(2)}, u32[]{:S(2)}) %collective-permute-start.1) | collective-permute-done | bytes 65568 | tf_op jit(solution)/shard_map/ppermute | solution.py:12
  22.5 1.9 %all_gather.12 = bf16[128,512]{1,0:T(8,128)(2,1)S(1)} all-gather(bf16[128,256]{1,0:T(8,128)(2,1)S(1)} %convolution_convert_fusion.3), channel_id=1, replica_groups=mesh['group'=2,'sub'=4,'tile'=2,'rep'=2] {'rep'}, dimensions={1}, use_global_device_ids=true | all-gather | bytes 196608 | tf_op jit(solution)/shard_map/all_gather | solution.py:65
  24.4 6.9 %all_gather.13 = bf16[256,512]{1,0:T(8,128)(2,1)S(1)} all-gather(bf16[128,512]{1,0:T(8,128)(2,1)S(1)} %all_gather.12), channel_id=1, replica_groups=mesh['group'=2,'sub'=4,'tile'=2,'rep'=2] {'tile'}, dimensions={0}, use_global_device_ids=true | all-gather | bytes 393216 | tf_op jit(solution)/shard_map/all_gather | solution.py:67
  32.5 20.2 %reduce-scatter.7.cloned.1.call-done = bf16[64,512]{1,0:T(8,128)(2,1)} async-done(((bf16[256,512]{1,0:T(8,128)(2,1)}), bf16[64,512]{1,0:T(8,128)(2,1)}) %reduce-scatter.7.cloned.1.call-update) | async-done | bytes 65552
  53.7 3.8 %all_to_all.38 = bf16[64,2,256]{2,0,1:T(8,128)(2,1)S(1)} all-to-all(bf16[64,2,256]{2,0,1:T(8,128)(2,1)S(1)} %copy.35), channel_id=1, replica_groups=mesh['group'=2,'sub'=4,'tile'=2,'rep'=2] {'rep'}, dimensions={1} | all-to-all | bytes 131072 | tf_op jit(solution)/shard_map/all_to_all | solution.py:72
  57.5 1.6 %convolution_add_fusion.1 = f32[1024,256]{0,1:T(8,128)S(1)} fusion(f32[1024,256]{0,1:T(8,128)} %copy-done.1, bf16[128,256]{1,0:T(8,128)(2,1)S(1)} %bitcast.78, bf16[1,1024,128]{2,1,0:T(8,128)(2,1)S(1)} %copy-done.4, pred[128]{0:T(512)(128)(4,1)S(1)} %iota_compare_fusion), kind=kOutput, calls=%fused_computation.11 | convolution fusion | flops 67502080 | bytes 2424960 | tf_op jit(solution)/shard_map/dot_general | solution.py:73
  59.1 1.0 copy.37
  60.1 2.5 %gather_fusion.3 = bf16[128,256]{1,0:T(8,128)(2,1)} fusion(bf16[1024,256]{1,0:T(8,128)(2,1)} %copy.37, s32[1024]{0:T(1024)S(1)} %pad_clamp_fusion), kind=kCustom, calls=%fused_computation.3 | custom fusion | bytes 131584 | tf_op jit(solution)/shard_map/gather | solution.py:47
  62.6 2.5 %gather_fusion.2 = bf16[128,256]{1,0:T(8,128)(2,1)} fusion(bf16[1024,256]{1,0:T(8,128)(2,1)} %copy.37, s32[1024]{0:T(1024)S(1)} %pad_clamp_fusion.1), kind=kCustom, calls=%fused_computation.2 | custom fusion | bytes 131584 | tf_op jit(solution)/shard_map/gather | solution.py:48
  65.0 3.4 %collective-permute-start.2 = (bf16[128,256]{1,0:T(8,128)(2,1)}, bf16[128,256]{1,0:T(8,128)(2,1)S(1)}, u32[]{:S(2)}, u32[]{:S(2)}) collective-permute-start(bf16[128,256]{1,0:T(8,128)(2,1)} %gather_fusion.2), channel_id=1, source_target_pairs={{0,2},{2,4},{4,6},{6,8},{8,10},{10,12},{12,14},{1,3},{3,5},{5,7},{... | collective-permute-start | bytes 196616 | tf_op jit(solution)/shard_map/ppermute | solution.py:12
  68.5 1.3 %collective-permute-start.3 = (bf16[128,256]{1,0:T(8,128)(2,1)}, bf16[128,256]{1,0:T(8,128)(2,1)S(1)}, u32[]{:S(2)}, u32[]{:S(2)}) collective-permute-start(bf16[128,256]{1,0:T(8,128)(2,1)} %gather_fusion.3), channel_id=1, source_target_pairs={{2,0},{4,2},{6,4},{8,6},{10,8},{12,10},{14,12},{3,1},{5,3},{7,5},{... | collective-permute-start | bytes 196616 | tf_op jit(solution)/shard_map/ppermute | solution.py:12
  70.7 4.2 %collective-permute-done.3 = bf16[128,256]{1,0:T(8,128)(2,1)S(1)} collective-permute-done((bf16[128,256]{1,0:T(8,128)(2,1)}, bf16[128,256]{1,0:T(8,128)(2,1)S(1)}, u32[]{:S(2)}, u32[]{:S(2)}) %collective-permute-start.3) | collective-permute-done | bytes 65568 | tf_op jit(solution)/shard_map/ppermute | solution.py:12
  74.9 1.1 add_convert_fusion.1
  75.9 1.8 %fusion.7 = f32[1024,256]{0,1:T(8,128)S(1)} fusion(bf16[1,1024,1024]{2,1,0:T(8,128)(2,1)S(1)} %copy-done, bf16[768,256]{1,0:T(8,128)(2,1)} %copy-done.7, bf16[128,256]{1,0:T(8,128)(2,1)S(1)} %get-tuple-element.6, bf16[128,256]{1,0:T(8,128)(2,1)S(1)} %get-tuple-element.5), kind=kOutput, calls=%fused_computation.9 | convolution fusion | flops 538443776 | bytes 3670016 | tf_op jit(solution)/shard_map/dot_general | solution.py:60
  78.7 1.9 %all_gather.14 = bf16[128,512]{1,0:T(8,128)(2,1)S(1)} all-gather(bf16[128,256]{1,0:T(8,128)(2,1)S(1)} %convolution_convert_fusion.2), channel_id=1, replica_groups=mesh['group'=2,'sub'=4,'tile'=2,'rep'=2] {'rep'}, dimensions={1}, use_global_device_ids=true | all-gather | bytes 196608 | tf_op jit(solution)/shard_map/all_gather | solution.py:65
  80.6 6.4 %all_gather.15 = bf16[256,512]{1,0:T(8,128)(2,1)S(1)} all-gather(bf16[128,512]{1,0:T(8,128)(2,1)S(1)} %all_gather.14), channel_id=1, replica_groups=mesh['group'=2,'sub'=4,'tile'=2,'rep'=2] {'tile'}, dimensions={0}, use_global_device_ids=true | all-gather | bytes 393216 | tf_op jit(solution)/shard_map/all_gather | solution.py:67
  87.9 1.8 %copy.51 = bf16[256,512]{1,0:T(8,128)(2,1)} copy(bf16[256,512]{0,1:T(8,128)(2,1)} %fusion.13) | data formatting | bytes 524288
  89.7 18.1 %reduce-scatter.9.cloned.1.call-done = bf16[64,512]{1,0:T(8,128)(2,1)} async-done(((bf16[256,512]{1,0:T(8,128)(2,1)}), bf16[64,512]{1,0:T(8,128)(2,1)}) %reduce-scatter.9.cloned.1.call-update) | async-done | bytes 65552
  109.5 4.7 %all_to_all.39 = bf16[64,2,256]{2,0,1:T(8,128)(2,1)S(1)} all-to-all(bf16[64,2,256]{2,0,1:T(8,128)(2,1)} %copy.40), channel_id=1, replica_groups=mesh['group'=2,'sub'=4,'tile'=2,'rep'=2] {'rep'}, dimensions={1} | all-to-all | bytes 131072 | tf_op jit(solution)/shard_map/all_to_all | solution.py:72
  114.2 1.1 fusion.11
  115.3 2.0 %copy.42 = bf16[1,1024,256]{2,1,0:T(8,128)(2,1)} copy(bf16[1,1024,256]{1,2,0:T(8,128)(2,1)} %fusion.11) | data formatting | bytes 1048576 | tf_op jit(solution)/shard_map/broadcast_in_dim | solution.py:76
  (44 shorter events, 12.4 us)
Async XLA Ops:
  6.5 13.8 %copy-start = (bf16[1,1024,1024]{2,1,0:T(8,128)(2,1)S(1)}, bf16[1,1024,1024]{2,1,0:T(8,128)(2,1)}, u32[]{:S(2)}) copy-start(bf16[1,1024,1024]{2,1,0:T(8,128)(2,1)} %param.8) | copy-start | bytes 6291460
  6.5 46.1 %reduce-scatter.7.cloned.1.call-start = ((), (), s32[]{:S(2)}) async-start(), calls=%async_computation.4 | async-start | bytes 327680
  8.3 9.6 %collective-permute-start = (bf16[128,256]{1,0:T(8,128)(2,1)S(1)}, bf16[128,256]{1,0:T(8,128)(2,1)S(1)}, u32[]{:S(2)}, u32[]{:S(2)}) collective-permute-start(bf16[128,256]{1,0:T(8,128)(2,1)S(1)} %gather_fusion), channel_id=1, source_target_pairs={{0,2},{2,4},{4,6},{6,8},{8,10},{10,12},{12,14},{1,3},{3,5},{5,7},{... | collective-permute-start | bytes 196616 | tf_op jit(solution)/shard_map/ppermute | solution.py:12
  14.0 6.2 %collective-permute-start.1 = (bf16[128,256]{1,0:T(8,128)(2,1)S(1)}, bf16[128,256]{1,0:T(8,128)(2,1)S(1)}, u32[]{:S(2)}, u32[]{:S(2)}) collective-permute-start(bf16[128,256]{1,0:T(8,128)(2,1)S(1)} %gather_fusion.1), channel_id=1, source_target_pairs={{2,0},{4,2},{6,4},{8,6},{10,8},{12,10},{14,12},{3,1},{5,3},{7,5},{... | collective-permute-start | bytes 196616 | tf_op jit(solution)/shard_map/ppermute | solution.py:12
  16.7 3.6 %copy-start.8 = (f32[128]{0:T(128)}, f32[128]{0:T(128)S(1)}, u32[]{:S(2)}) copy-start(f32[128]{0:T(128)S(1)} %get-tuple-element.10) | copy-start | bytes 1540
  17.8 2.5 %copy-start.5 = (f32[1,1024,256]{2,1,0:T(8,128)}, f32[1,1024,256]{2,1,0:T(8,128)S(1)}, u32[]{:S(2)}) copy-start(f32[1,1024,256]{2,1,0:T(8,128)S(1)} %convert_element_type.57) | copy-start | bytes 3145732
  17.9 3.2 %copy-start.7 = (bf16[768,256]{1,0:T(8,128)(2,1)}, bf16[768,256]{1,0:T(8,128)(2,1)S(1)}, u32[]{:S(2)}) copy-start(bf16[768,256]{1,0:T(8,128)(2,1)S(1)} %fusion.23) | copy-start | bytes 1179652
  20.3 1.8 %copy-start.4 = (bf16[1,1024,128]{2,1,0:T(8,128)(2,1)S(1)}, bf16[1,1024,128]{2,1,0:T(8,128)(2,1)}, u32[]{:S(2)}) copy-start(bf16[1,1024,128]{2,1,0:T(8,128)(2,1)} %param.11) | copy-start | bytes 786436
  20.3 10.9 %copy-start.6 = (bf16[4,1,64,1,256]{4,2,3,1,0:T(8,128)(2,1)S(1)}, bf16[4,1,64,1,256]{4,2,3,1,0:T(8,128)(2,1)}, u32[]{:S(2)}) copy-start(bf16[4,1,64,1,256]{4,2,3,1,0:T(8,128)(2,1)} %param.13) | copy-start | bytes 393220
  21.1 1.0 copy-start.1
  32.4 75.4 %reduce-scatter.9.cloned.1.call-start = ((), (), s32[]{:S(2)}) async-start(), calls=%async_computation.5 | async-start | bytes 327680
  65.0 5.6 %collective-permute-start.2 = (bf16[128,256]{1,0:T(8,128)(2,1)}, bf16[128,256]{1,0:T(8,128)(2,1)S(1)}, u32[]{:S(2)}, u32[]{:S(2)}) collective-permute-start(bf16[128,256]{1,0:T(8,128)(2,1)} %gather_fusion.2), channel_id=1, source_target_pairs={{0,2},{2,4},{4,6},{6,8},{8,10},{10,12},{12,14},{1,3},{3,5},{5,7},{... | collective-permute-start | bytes 196616 | tf_op jit(solution)/shard_map/ppermute | solution.py:12
  68.5 6.4 %collective-permute-start.3 = (bf16[128,256]{1,0:T(8,128)(2,1)}, bf16[128,256]{1,0:T(8,128)(2,1)S(1)}, u32[]{:S(2)}, u32[]{:S(2)}) collective-permute-start(bf16[128,256]{1,0:T(8,128)(2,1)} %gather_fusion.3), channel_id=1, source_target_pairs={{2,0},{4,2},{6,4},{8,6},{10,8},{12,10},{14,12},{3,1},{5,3},{7,5},{... | collective-permute-start | bytes 196616 | tf_op jit(solution)/shard_map/ppermute | solution.py:12
  77.7 1.0 copy-start.2
  80.6 33.6 %copy-start.3 = (f32[1024,256]{0,1:T(8,128)S(1)}, f32[1024,256]{0,1:T(8,128)}, u32[]{:S(2)}) copy-start(f32[1024,256]{0,1:T(8,128)} %copy-done.2) | copy-start | bytes 3145732
Sparse Core Ops, SparseCore 0:
  32.5 20.0 reduce-scatter.6
  89.9 17.9 reduce-scatter.8
where the time goes:
time: 125 us; the launch traced here: 124 us
  waiting for transfers between devices  45.6 us (36%)
  blocking collectives  25.5 us (20%)
  local copies, waits for them, and re-layouts  17.6 us (14%)
  between operations  14.3 us (11%)
  starting transfers between devices  10.9 us (9%)
  matrix products  7.14 us (6%)
  other arithmetic  3.16 us (3%)
    unnamed x4, waiting for transfers between devices  38.3 us
    all_gather x2, blocking collectives, local(): lax.all_gather(all_modes, 'tile', axis=0, tiled=True)  13.3 us
    ppermute x4, starting transfers between devices, passed_along(): return lax.ppermute(shard, axis, pairs)  10.9 us
    all_to_all x2, blocking collectives, local(): lax.all_to_all(own_coarse, 'rep', split_axis=1, concat_axis=0, tiled=True)  8.49 us
    ppermute x4, waiting for transfers between devices, passed_along(): return lax.ppermute(shard, axis, pairs)  7.31 us
    unnamed x22, local copies, waits for them, and re-layouts  6.19 us
    all_gather x2, blocking collectives, local(): all_modes = lax.all_gather(projected, 'rep', axis=1, tiled=True)  3.79 us
    gather x2, local copies, waits for them, and re-layouts, local(): upper_trace = iterate[trace_rows[0, 1]]  3.33 us
  transfers between devices with their start and end apart: 6, of which 5 were waited for; matrix products, arithmetic and copies ran while one was open for 2% of the time, Pallas kernels for 0%

commit v1 on v0

--- a/solution.py
+++ b/solution.py
@@ -69,7 +69,12 @@
         own_coarse = lax.psum_scatter(
             partial_value.astype(jnp.bfloat16), "sub", scatter_dimension=0, tiled=True
         )
-        coarse_rows = lax.all_to_all(own_coarse, "rep", split_axis=1, concat_axis=0, tiled=True)
+        coarse_rows = jnp.concatenate(
+            lax.all_to_all(
+                jnp.stack(jnp.split(own_coarse, lax.axis_size("rep"), axis=1)), "rep", 0, 0
+            ),
+            axis=0,
+        )
         iterate = local_solve + jnp.dot(
             masked_basis, coarse_rows, preferred_element_type=jnp.float32
         )

time: 125 us -> 127 us (1.016)
  local copies, waits for them, and re-layouts: 17.6 us -> 18.9 us
    split x0 -> x2, local copies, waits for them, and re-layouts: none -> 1.56 us  [local(): jnp.split(own_coarse, lax.axis_size('rep'), axis=1)]
    unnamed x22 -> x24, local copies, waits for them, and re-layouts: 6.19 us -> 5.94 us
where the time goes in v1:
time: 127 us; the launch traced here: 126 us
  waiting for transfers between devices  45.6 us (36%)
  blocking collectives  25.5 us (20%)
  local copies, waits for them, and re-layouts  18.9 us (15%)
  between operations  14.3 us (11%)
  starting transfers between devices  10.9 us (9%)
  matrix products  7.15 us (6%)
  other arithmetic  4.09 us (3%)
    unnamed x4, waiting for transfers between devices  38.3 us
    all_gather x2, blocking collectives, local(): lax.all_gather(all_modes, 'tile', axis=0, tiled=True)  13.3 us
    ppermute x4, starting transfers between devices, passed_along(): return lax.ppermute(shard, axis, pairs)  10.9 us
    all_to_all x2, blocking collectives, local(): lax.all_to_all(jnp.stack(jnp.split(own_coarse, lax.axis_size('rep'), axis...  8.49 us
    ppermute x4, waiting for transfers between devices, passed_along(): return lax.ppermute(shard, axis, pairs)  7.31 us
    unnamed x24, local copies, waits for them, and re-layouts  5.94 us
    all_gather x2, blocking collectives, local(): all_modes = lax.all_gather(projected, 'rep', axis=1, tiled=True)  3.79 us
    gather x2, local copies, waits for them, and re-layouts, local(): upper_trace = iterate[trace_rows[0, 1]]  3.33 us
  transfers between devices with their start and end apart: 6, of which 5 were waited for; matrix products, arithmetic and copies ran while one was open for 2% of the time, Pallas kernels for 0%

profile of v1, /device:TPU:0, one launch (start us, length us, event | category | flops | bytes accessed | tf_op | source)
XLA Modules:
  0.0 126.4 jit_solution(7237585949638254386)
XLA Ops:
  8.3 4.8 %collective-permute-start = (bf16[128,256]{1,0:T(8,128)(2,1)S(1)}, bf16[128,256]{1,0:T(8,128)(2,1)S(1)}, u32[]{:S(2)}, u32[]{:S(2)}) collective-permute-start(bf16[128,256]{1,0:T(8,128)(2,1)S(1)} %gather_fusion), channel_id=1, source_target_pairs={{0,2},{2,4},{4,6},{6,8},{8,10},{10,12},{12,14},{1,3},{3,5},{5,7},{... | collective-permute-start | bytes 196616 | tf_op jit(solution)/shard_map/ppermute | solution.py:12
  14.0 1.3 %collective-permute-start.1 = (bf16[128,256]{1,0:T(8,128)(2,1)S(1)}, bf16[128,256]{1,0:T(8,128)(2,1)S(1)}, u32[]{:S(2)}, u32[]{:S(2)}) collective-permute-start(bf16[128,256]{1,0:T(8,128)(2,1)S(1)} %gather_fusion.1), channel_id=1, source_target_pairs={{2,0},{4,2},{6,4},{8,6},{10,8},{12,10},{14,12},{3,1},{5,3},{7,5},{... | collective-permute-start | bytes 196616 | tf_op jit(solution)/shard_map/ppermute | solution.py:12
  16.7 1.1 convert_element_type.57
  17.9 2.2 %collective-permute-done.1 = bf16[128,256]{1,0:T(8,128)(2,1)S(1)} collective-permute-done((bf16[128,256]{1,0:T(8,128)(2,1)S(1)}, bf16[128,256]{1,0:T(8,128)(2,1)S(1)}, u32[]{:S(2)}, u32[]{:S(2)}) %collective-permute-start.1) | collective-permute-done | bytes 65568 | tf_op jit(solution)/shard_map/ppermute | solution.py:12
  22.4 1.9 %all_gather.12 = bf16[128,512]{1,0:T(8,128)(2,1)S(1)} all-gather(bf16[128,256]{1,0:T(8,128)(2,1)S(1)} %convolution_convert_fusion.3), channel_id=1, replica_groups=mesh['group'=2,'sub'=4,'tile'=2,'rep'=2] {'rep'}, dimensions={1}, use_global_device_ids=true | all-gather | bytes 196608 | tf_op jit(solution)/shard_map/all_gather | solution.py:65
  24.3 6.9 %all_gather.13 = bf16[256,512]{1,0:T(8,128)(2,1)S(1)} all-gather(bf16[128,512]{1,0:T(8,128)(2,1)S(1)} %all_gather.12), channel_id=1, replica_groups=mesh['group'=2,'sub'=4,'tile'=2,'rep'=2] {'tile'}, dimensions={0}, use_global_device_ids=true | all-gather | bytes 393216 | tf_op jit(solution)/shard_map/all_gather | solution.py:67
  32.4 20.2 %reduce-scatter.7.cloned.1.call-done = bf16[64,512]{1,0:T(8,128)(2,1)} async-done(((bf16[256,512]{1,0:T(8,128)(2,1)}), bf16[64,512]{1,0:T(8,128)(2,1)}) %reduce-scatter.7.cloned.1.call-update) | async-done | bytes 65552
  53.8 3.8 %all_to_all.10 = bf16[2,64,256]{2,1,0:T(8,128)(2,1)S(1)} all-to-all(bf16[2,64,256]{2,1,0:T(8,128)(2,1)S(1)} %copy.20), channel_id=1, replica_groups=mesh['group'=2,'sub'=4,'tile'=2,'rep'=2] {'rep'}, dimensions={0} | all-to-all | bytes 131072 | tf_op jit(solution)/shard_map/all_to_all | solution.py:73
  57.6 1.6 %convolution_add_fusion.1 = f32[1024,256]{0,1:T(8,128)S(1)} fusion(f32[1024,256]{0,1:T(8,128)} %copy-done.1, bf16[128,256]{1,0:T(8,128)(2,1)S(1)} %bitcast.78, bf16[1,1024,128]{2,1,0:T(8,128)(2,1)S(1)} %copy-done.4, pred[128]{0:T(512)(128)(4,1)S(1)} %iota_compare_fusion), kind=kOutput, calls=%fused_computation.11 | convolution fusion | flops 67502080 | bytes 2424960 | tf_op jit(solution)/shard_map/dot_general | solution.py:78
  59.2 1.0 copy.22
  60.2 2.5 %gather_fusion.3 = bf16[128,256]{1,0:T(8,128)(2,1)} fusion(bf16[1024,256]{1,0:T(8,128)(2,1)} %copy.22, s32[1024]{0:T(1024)S(1)} %pad_clamp_fusion), kind=kCustom, calls=%fused_computation.3 | custom fusion | bytes 131584 | tf_op jit(solution)/shard_map/gather | solution.py:47
  62.6 2.5 %gather_fusion.2 = bf16[128,256]{1,0:T(8,128)(2,1)} fusion(bf16[1024,256]{1,0:T(8,128)(2,1)} %copy.22, s32[1024]{0:T(1024)S(1)} %pad_clamp_fusion.1), kind=kCustom, calls=%fused_computation.2 | custom fusion | bytes 131584 | tf_op jit(solution)/shard_map/gather | solution.py:48
  65.1 3.5 %collective-permute-start.2 = (bf16[128,256]{1,0:T(8,128)(2,1)}, bf16[128,256]{1,0:T(8,128)(2,1)S(1)}, u32[]{:S(2)}, u32[]{:S(2)}) collective-permute-start(bf16[128,256]{1,0:T(8,128)(2,1)} %gather_fusion.2), channel_id=1, source_target_pairs={{0,2},{2,4},{4,6},{6,8},{8,10},{10,12},{12,14},{1,3},{3,5},{5,7},{... | collective-permute-start | bytes 196616 | tf_op jit(solution)/shard_map/ppermute | solution.py:12
  68.6 1.3 %collective-permute-start.3 = (bf16[128,256]{1,0:T(8,128)(2,1)}, bf16[128,256]{1,0:T(8,128)(2,1)S(1)}, u32[]{:S(2)}, u32[]{:S(2)}) collective-permute-start(bf16[128,256]{1,0:T(8,128)(2,1)} %gather_fusion.3), channel_id=1, source_target_pairs={{2,0},{4,2},{6,4},{8,6},{10,8},{12,10},{14,12},{3,1},{5,3},{7,5},{... | collective-permute-start | bytes 196616 | tf_op jit(solution)/shard_map/ppermute | solution.py:12
  70.8 4.2 %collective-permute-done.3 = bf16[128,256]{1,0:T(8,128)(2,1)S(1)} collective-permute-done((bf16[128,256]{1,0:T(8,128)(2,1)}, bf16[128,256]{1,0:T(8,128)(2,1)S(1)}, u32[]{:S(2)}, u32[]{:S(2)}) %collective-permute-start.3) | collective-permute-done | bytes 65568 | tf_op jit(solution)/shard_map/ppermute | solution.py:12
  75.0 1.1 add_convert_fusion.1
  76.0 1.8 %fusion.7 = f32[1024,256]{0,1:T(8,128)S(1)} fusion(bf16[1,1024,1024]{2,1,0:T(8,128)(2,1)S(1)} %copy-done, bf16[768,256]{1,0:T(8,128)(2,1)} %copy-done.7, bf16[128,256]{1,0:T(8,128)(2,1)S(1)} %get-tuple-element.6, bf16[128,256]{1,0:T(8,128)(2,1)S(1)} %get-tuple-element.5), kind=kOutput, calls=%fused_computation.9 | convolution fusion | flops 538443776 | bytes 3670016 | tf_op jit(solution)/shard_map/dot_general | solution.py:60
  78.8 1.9 %all_gather.14 = bf16[128,512]{1,0:T(8,128)(2,1)S(1)} all-gather(bf16[128,256]{1,0:T(8,128)(2,1)S(1)} %convolution_convert_fusion.2), channel_id=1, replica_groups=mesh['group'=2,'sub'=4,'tile'=2,'rep'=2] {'rep'}, dimensions={1}, use_global_device_ids=true | all-gather | bytes 196608 | tf_op jit(solution)/shard_map/all_gather | solution.py:65
  80.7 6.4 %all_gather.15 = bf16[256,512]{1,0:T(8,128)(2,1)S(1)} all-gather(bf16[128,512]{1,0:T(8,128)(2,1)S(1)} %all_gather.14), channel_id=1, replica_groups=mesh['group'=2,'sub'=4,'tile'=2,'rep'=2] {'tile'}, dimensions={0}, use_global_device_ids=true | all-gather | bytes 393216 | tf_op jit(solution)/shard_map/all_gather | solution.py:67
  88.0 1.8 %copy.31 = bf16[256,512]{1,0:T(8,128)(2,1)} copy(bf16[256,512]{0,1:T(8,128)(2,1)} %fusion.13) | data formatting | bytes 524288
  89.8 18.0 %reduce-scatter.9.cloned.1.call-done = bf16[64,512]{1,0:T(8,128)(2,1)} async-done(((bf16[256,512]{1,0:T(8,128)(2,1)}), bf16[64,512]{1,0:T(8,128)(2,1)}) %reduce-scatter.9.cloned.1.call-update) | async-done | bytes 65552
  111.7 4.7 %all_to_all.11 = bf16[2,64,256]{2,1,0:T(8,128)(2,1)S(1)} all-to-all(bf16[2,64,256]{2,1,0:T(8,128)(2,1)} %copy.24), channel_id=1, replica_groups=mesh['group'=2,'sub'=4,'tile'=2,'rep'=2] {'rep'}, dimensions={0} | all-to-all | bytes 131072 | tf_op jit(solution)/shard_map/all_to_all | solution.py:73
  116.4 1.1 fusion.11
  117.6 2.0 %copy.26 = bf16[1,1024,256]{2,1,0:T(8,128)(2,1)} copy(bf16[1,1024,256]{1,2,0:T(8,128)(2,1)} %fusion.11) | data formatting | bytes 1048576 | tf_op jit(solution)/shard_map/broadcast_in_dim | solution.py:81
  (50 shorter events, 14.6 us)
Async XLA Ops:
  6.5 13.8 %copy-start = (bf16[1,1024,1024]{2,1,0:T(8,128)(2,1)S(1)}, bf16[1,1024,1024]{2,1,0:T(8,128)(2,1)}, u32[]{:S(2)}) copy-start(bf16[1,1024,1024]{2,1,0:T(8,128)(2,1)} %param.8) | copy-start | bytes 6291460
  6.5 46.1 %reduce-scatter.7.cloned.1.call-start = ((), (), s32[]{:S(2)}) async-start(), calls=%async_computation.4 | async-start | bytes 327680
  8.3 9.6 %collective-permute-start = (bf16[128,256]{1,0:T(8,128)(2,1)S(1)}, bf16[128,256]{1,0:T(8,128)(2,1)S(1)}, u32[]{:S(2)}, u32[]{:S(2)}) collective-permute-start(bf16[128,256]{1,0:T(8,128)(2,1)S(1)} %gather_fusion), channel_id=1, source_target_pairs={{0,2},{2,4},{4,6},{6,8},{8,10},{10,12},{12,14},{1,3},{3,5},{5,7},{... | collective-permute-start | bytes 196616 | tf_op jit(solution)/shard_map/ppermute | solution.py:12
  14.0 6.2 %collective-permute-start.1 = (bf16[128,256]{1,0:T(8,128)(2,1)S(1)}, bf16[128,256]{1,0:T(8,128)(2,1)S(1)}, u32[]{:S(2)}, u32[]{:S(2)}) collective-permute-start(bf16[128,256]{1,0:T(8,128)(2,1)S(1)} %gather_fusion.1), channel_id=1, source_target_pairs={{2,0},{4,2},{6,4},{8,6},{10,8},{12,10},{14,12},{3,1},{5,3},{7,5},{... | collective-permute-start | bytes 196616 | tf_op jit(solution)/shard_map/ppermute | solution.py:12
  16.7 3.6 %copy-start.8 = (f32[128]{0:T(128)}, f32[128]{0:T(128)S(1)}, u32[]{:S(2)}) copy-start(f32[128]{0:T(128)S(1)} %get-tuple-element.14) | copy-start | bytes 1540
  17.8 2.5 %copy-start.5 = (f32[1,1024,256]{2,1,0:T(8,128)}, f32[1,1024,256]{2,1,0:T(8,128)S(1)}, u32[]{:S(2)}) copy-start(f32[1,1024,256]{2,1,0:T(8,128)S(1)} %convert_element_type.57) | copy-start | bytes 3145732
  17.9 3.2 %copy-start.7 = (bf16[768,256]{1,0:T(8,128)(2,1)}, bf16[768,256]{1,0:T(8,128)(2,1)S(1)}, u32[]{:S(2)}) copy-start(bf16[768,256]{1,0:T(8,128)(2,1)S(1)} %fusion.23) | copy-start | bytes 1179652
  20.3 1.8 %copy-start.4 = (bf16[1,1024,128]{2,1,0:T(8,128)(2,1)S(1)}, bf16[1,1024,128]{2,1,0:T(8,128)(2,1)}, u32[]{:S(2)}) copy-start(bf16[1,1024,128]{2,1,0:T(8,128)(2,1)} %param.11) | copy-start | bytes 786436
  20.3 10.9 %copy-start.6 = (bf16[4,1,64,1,256]{4,2,3,1,0:T(8,128)(2,1)S(1)}, bf16[4,1,64,1,256]{4,2,3,1,0:T(8,128)(2,1)}, u32[]{:S(2)}) copy-start(bf16[4,1,64,1,256]{4,2,3,1,0:T(8,128)(2,1)} %param.13) | copy-start | bytes 393220
  21.1 1.0 copy-start.1
  32.4 75.5 %reduce-scatter.9.cloned.1.call-start = ((), (), s32[]{:S(2)}) async-start(), calls=%async_computation.5 | async-start | bytes 327680
  65.1 5.7 %collective-permute-start.2 = (bf16[128,256]{1,0:T(8,128)(2,1)}, bf16[128,256]{1,0:T(8,128)(2,1)S(1)}, u32[]{:S(2)}, u32[]{:S(2)}) collective-permute-start(bf16[128,256]{1,0:T(8,128)(2,1)} %gather_fusion.2), channel_id=1, source_target_pairs={{0,2},{2,4},{4,6},{6,8},{8,10},{10,12},{12,14},{1,3},{3,5},{5,7},{... | collective-permute-start | bytes 196616 | tf_op jit(solution)/shard_map/ppermute | solution.py:12
  68.6 6.4 %collective-permute-start.3 = (bf16[128,256]{1,0:T(8,128)(2,1)}, bf16[128,256]{1,0:T(8,128)(2,1)S(1)}, u32[]{:S(2)}, u32[]{:S(2)}) collective-permute-start(bf16[128,256]{1,0:T(8,128)(2,1)} %gather_fusion.3), channel_id=1, source_target_pairs={{2,0},{4,2},{6,4},{8,6},{10,8},{12,10},{14,12},{3,1},{5,3},{7,5},{... | collective-permute-start | bytes 196616 | tf_op jit(solution)/shard_map/ppermute | solution.py:12
  77.8 1.0 copy-start.2
  80.7 35.8 %copy-start.3 = (f32[1024,256]{0,1:T(8,128)S(1)}, f32[1024,256]{0,1:T(8,128)}, u32[]{:S(2)}) copy-start(f32[1024,256]{0,1:T(8,128)} %copy-done.2) | copy-start | bytes 3145732
Sparse Core Ops, SparseCore 0:
  32.5 20.0 reduce-scatter.6
  90.0 17.8 reduce-scatter.8
